TPU v7x, 256 devices: a whole 4x4x8 slice. The times are simulated.
256 devices in a mesh: opair: 8 (over y, core), vpair: 32 (over z, x).
Axes of the slice: x: 4, y: 4, z: 8, core: 2. Of those that a mesh axis runs over, the one named last changes fastest.
Arguments:
- amplitudes: bfloat16 [1600, 24, 1000], P('vpair', 'opair'), may hold values from -6 to 6
- ladder_ints: bfloat16 [24, 1000, 32, 1000], P('opair', None, 'vpair'), may hold values from -0.0390625 to 0.0390625
- cycle_amps: bfloat16 [24, 100, 512], P('opair'), may hold values from -6 to 6
- cycle_ints: bfloat16 [24, 100, 100000], P('opair', None, 'vpair'), may hold values from -0.125 to 0.125
- occ_blocks: int32 [8], replicated, may hold values from 1 to 33, 100 in all
- virt_blocks: int32 [8], replicated, may hold values from 1 to 250, 1000 in all
- occ_start: int32 [1], replicated, may hold values from 0 to 84
- virt_start: int32 [1], replicated, may hold values from 0 to 968
- eps_occ: float32 [100], replicated, may hold values from -1 to -0.25
- eps_virt: float32 [1000], replicated, may hold values from 0.25 to 1.5
Outputs:
- update: float32 [16, 32, 100, 1000], P('opair', 'vpair')
All inputs are finite; a program needn't handle non-finite values.
Results may differ from a plain program's by a relative error of at most 0.0004.
Values may be sent and summed in bfloat16 or wider, within the bound.
No kernel may reach another device: no remote copies, remote signals or barrier semaphores. Data moves between devices by JAX's collectives and lax.ppermute only.
A program may use at most 128 MiB of HBM per device.

v0:
```python
import jax
import jax.numpy as jnp
from jax import lax
from jax.sharding import PartitionSpec as P

NO = 100
NV = 1000
I_DEV = 2
A_DEV = 1
N_CHUNK = 2


def irrep_of(blocks, index):
    bounds = jnp.cumsum(blocks)[:-1]
    return jnp.sum((index[:, None] >= bounds[None, :]).astype(jnp.int32), axis=1)


def shards(
    amplitudes,
    ladder_ints,
    cycle_amps,
    cycle_ints,
    occ_blocks,
    virt_blocks,
    occ_start,
    virt_start,
    eps_occ,
    eps_virt,
):
    i_win = I_DEV * lax.axis_size("opair")
    a_win = A_DEV * lax.axis_size("vpair")
    slab_depth = ladder_ints.shape[0] * ladder_ints.shape[1]
    jb_dev = cycle_ints.shape[2]
    cycle = lax.dot_general(
        cycle_amps, cycle_ints, (((0, 1), (0, 1)), ((), ())), preferred_element_type=jnp.float32
    )
    cycle_part = cycle.reshape(i_win, a_win, jb_dev)
    c_dev = ladder_ints.shape[0]
    v_slab = ladder_ints.reshape(c_dev, ladder_ints.shape[1], A_DEV * NV)
    p_dev = amplitudes.shape[0]
    p_chunk = p_dev // N_CHUNK
    parts = []
    prev = None
    for s in range(N_CHUNK):
        loc = amplitudes[s * p_chunk : (s + 1) * p_chunk].transpose(1, 0, 2)
        if prev is None:
            loc, cycle_part = lax.optimization_barrier((loc, cycle_part))
            cycle = lax.psum_scatter(cycle_part, "opair", scatter_dimension=0, tiled=True)
        elif s == 1:
            loc, _, cycle = lax.optimization_barrier((loc, prev, cycle))
        else:
            loc, _ = lax.optimization_barrier((loc, prev))
        piece = lax.all_gather(loc, "vpair", axis=1, tiled=True)
        prev = piece
        part = lax.dot_general(
            piece, v_slab, (((0, 2), (0, 1)), ((), ())), preferred_element_type=jnp.float32
        )
        part = part.reshape(i_win, NO // N_CHUNK, A_DEV * NV)
        if s == 1:
            cycle = lax.all_to_all(cycle, "vpair", split_axis=1, concat_axis=2, tiled=True)
            part, parts[-1], cycle = lax.optimization_barrier((part, parts[-1], cycle))
        elif parts:
            part, parts[-1] = lax.optimization_barrier((part, parts[-1]))
        parts.append(lax.psum_scatter(part, "opair", scatter_dimension=0, tiled=True))
    parts = [q.reshape(I_DEV, NO // p_dev, p_chunk, A_DEV * NV) for q in parts]
    ladder = jnp.stack(parts, axis=2).reshape(I_DEV, NO, A_DEV * NV)
    resid = ladder.reshape(I_DEV, NO, A_DEV, NV).transpose(0, 2, 1, 3) + cycle.reshape(
        I_DEV, A_DEV, NO, NV
    )
    first_occ = occ_start[0] + lax.axis_index("opair") * I_DEV
    first_virt = virt_start[0] + lax.axis_index("vpair") * A_DEV
    glob_i = first_occ + jnp.arange(I_DEV, dtype=jnp.int32)
    glob_a = first_virt + jnp.arange(A_DEV, dtype=jnp.int32)
    sym_i = irrep_of(occ_blocks, glob_i)
    sym_a = irrep_of(virt_blocks, glob_a)
    sym_j = irrep_of(occ_blocks, jnp.arange(NO, dtype=jnp.int32))
    sym_b = irrep_of(virt_blocks, jnp.arange(NV, dtype=jnp.int32))
    total_sym = jnp.bitwise_xor(
        jnp.bitwise_xor(sym_i[:, None, None, None], sym_a[None, :, None, None]),
        jnp.bitwise_xor(sym_j[None, None, :, None], sym_b[None, None, None, :]),
    )
    e_i = lax.dynamic_slice_in_dim(eps_occ, first_occ, I_DEV)
    e_a = lax.dynamic_slice_in_dim(eps_virt, first_virt, A_DEV)
    denom = (
        e_i[:, None, None, None]
        - e_a[None, :, None, None]
        + eps_occ[None, None, :, None]
        - eps_virt[None, None, None, :]
    )
    return jnp.where(total_sym == 0, resid / denom, jnp.float32(0.0))


def solution(mesh):
    placed = (
        P("vpair", "opair", None),
        P("opair", None, "vpair", None),
        P("opair", None, None),
        P("opair", None, "vpair"),
        P(),
        P(),
        P(),
        P(),
        P(),
        P(),
    )
    return jax.shard_map(
        shards,
        mesh=mesh,
        in_specs=placed,
        out_specs=P("opair", "vpair", None, None),
        check_vma=False,
    )
```

profile of v0, /device:TPU:2, one launch (start us, length us, event | category | flops | bytes accessed | tf_op | source)
XLA Modules:
  0.0 265.2 jit_solution(7617233664805227034)
XLA Ops:
  7.4 1.2 fusion.19
  8.6 0.8 copy.72
  9.4 5.7 %fusion.20 = f32[512,3125,1]{1,0,2:T(8,128)} fusion(bf16[3,100,512]{2,1,0:T(8,128)(2,1)} %param.12, bf16[3,100,3125]{2,1,0:T(8,128)(2,1)S(1)} %copy-done), kind=kOutput, calls=%fused_computation.30 | convolution fusion | flops 960000000 | bytes 8582200 | tf_op jit(solution)/shard_map/dot_general | solution.py:34
  15.2 0.5 reduce-scatter.4.cloned.1.call-update
  15.7 0.8 copy.73
  16.6 89.8 %all-gather.3.cloned.1.call-done = bf16[3,800,1000]{2,0,1:T(4,128)(2,1)} async-done(((bf16[3,25,1000]{2,0,1:T(4,128)(2,1)}), bf16[3,800,1000]{2,0,1:T(4,128)(2,1)}) %all-gather.3.cloned.1.call-update) | async-done | bytes 4800016 | tf_op jit(solution)/shard_map/all_gather | solution.py:53
  106.5 13.3 %fusion.11 = f32[16,50,1000]{2,1,0:T(8,128)} fusion(bf16[3,1000,1,1000]{3,1,2,0:T(8,128)(2,1)} %param.11, bf16[16,50,3,1000]{3,2,1,0:T(4,128)(2,1)} %bitcast.55), kind=kOutput, calls=%fused_computation.7 | convolution fusion | flops 4800000000 | bytes 14000000 | tf_op jit(solution)/shard_map/dot_general | solution.py:55
  119.9 0.6 copy.43
  120.5 34.7 %all_to_all.12 = f32[2,32,3125]{2,0,1:T(2,128)S(1)} all-to-all(f32[2,32,3125]{2,0,1:T(2,128)S(1)} %copy.43), channel_id=1, replica_groups=mesh['opair'=8,'vpair'=32] {'vpair'}, dimensions={1} | all-to-all | bytes 1600000 | tf_op jit(solution)/shard_map/all_to_all | solution.py:60
  155.3 2.0 all_to_all.10
  157.3 43.4 %all-gather.5.cloned.1.call-done = bf16[3,800,1000]{2,0,1:T(4,128)(2,1)} async-done(((bf16[3,25,1000]{2,0,1:T(4,128)(2,1)}), bf16[3,800,1000]{2,0,1:T(4,128)(2,1)}) %all-gather.5.cloned.1.call-update) | async-done | bytes 4800016 | tf_op jit(solution)/shard_map/all_gather | solution.py:53
  200.7 13.3 %fusion.6 = f32[16,50,1000]{2,1,0:T(8,128)} fusion(bf16[3,1000,1,1000]{3,1,2,0:T(8,128)(2,1)} %param.11, bf16[16,50,3,1000]{3,2,1,0:T(4,128)(2,1)} %bitcast.56), kind=kOutput, calls=%fused_computation.6 | convolution fusion | flops 4800000000 | bytes 14000000 | tf_op jit(solution)/shard_map/dot_general | solution.py:55
  215.3 0.2 reduce-window.6
  215.7 0.6 dynamic_slice.7
  216.4 0.7 dynamic-slice_subtract_fusion
  217.1 0.7 fusion.18
  218.2 0.7 broadcast_xor_fusion.1
  219.1 2.1 copy.45
  221.1 2.2 reshape.185
  223.3 28.6 %reduce-scatter.8.cloned.1.call-done = f32[2,50,1000]{2,1,0:T(8,128)} async-done(((f32[16,50,1000]{2,1,0:T(8,128)}), f32[2,50,1000]{2,1,0:T(8,128)}) %reduce-scatter.8.cloned.1.call-update) | async-done | bytes 400016 | tf_op jit(solution)/shard_map/reduce_scatter | solution.py:64
  252.0 1.3 copy.46
  253.3 1.4 pad_maximum_fusion
  254.8 1.1 compare_select_fusion
  255.9 1.7 copy.49
  (33 shorter events, 1.1 us)
Async XLA Ops:
  7.4 2.0 copy-start
  7.4 99.0 %all-gather.3.cloned.1.call-start = ((), (), s32[]{:S(2)}) async-start(), calls=%async_computation.4 | async-start | bytes 6758400 | tf_op jit(solution)/shard_map/all_gather | solution.py:53
  15.1 91.3 %reduce-scatter.4.cloned.1.call-start = ((), (), s32[]{:S(2)}) async-start(), calls=%async_computation.5 | async-start | bytes 7372800 | tf_op jit(solution)/shard_map/reduce_scatter | solution.py:48
  15.7 185.0 %all-gather.5.cloned.1.call-start = ((), (), s32[]{:S(2)}) async-start(), calls=%async_computation.6 | async-start | bytes 6758400 | tf_op jit(solution)/shard_map/all_gather | solution.py:53
  106.4 107.6 %reduce-scatter.6.cloned.1.call-start = ((), (), s32[]{:S(2)}) async-start(), calls=%async_computation.7 | async-start | bytes 4128768 | tf_op jit(solution)/shard_map/reduce_scatter | solution.py:64
  106.5 13.4 %copy-start.1 = (f32[2,32,3125]{2,1,0:T(8,128)S(1)}, f32[2,32,3125]{2,1,0:T(8,128)}, u32[]{:S(2)}) copy-start(f32[2,32,3125]{2,1,0:T(8,128)} %reduce-scatter.4.cloned.1.call-done) | copy-start | bytes 2400004
  119.8 132.2 %reduce-scatter.8.cloned.1.call-start = ((), (), s32[]{:S(2)}) async-start(), calls=%async_computation.8 | async-start | bytes 4128768 | tf_op jit(solution)/shard_map/reduce_scatter | solution.py:64
  200.7 14.7 %copy-start.4 = (s32[8]{0:T(128)S(1)}, s32[8]{0:T(128)}, u32[]{:S(2)}) copy-start(s32[8]{0:T(128)} %param.14) | copy-start | bytes 100
  200.7 14.9 %copy-start.5 = (s32[8]{0:T(128)S(1)}, s32[8]{0:T(128)}, u32[]{:S(2)}) copy-start(s32[8]{0:T(128)} %param.15) | copy-start | bytes 100
  200.7 15.1 %copy-start.2 = (f32[1000]{0:T(1024)S(1)}, f32[1000]{0:T(1024)}, u32[]{:S(2)}) copy-start(f32[1000]{0:T(1024)} %param.19) | copy-start | bytes 12004
  200.7 15.7 %copy-start.3 = (f32[100]{0:T(128)S(1)}, f32[100]{0:T(128)}, u32[]{:S(2)}) copy-start(f32[100]{0:T(128)} %param.18) | copy-start | bytes 1204
Sparse Core Ops, SparseCore 0:
  15.2 91.1 all-gather.2
  109.0 91.6 all-gather.4
Sparse Core Ops, SparseCore 1:
  18.2 49.4 reduce-scatter.3
  119.9 38.6 reduce-scatter.5
  214.1 37.8 reduce-scatter.7
where the time goes:
time: 266 us; the launch traced here: 265 us
  waiting for transfers between devices  162 us (61%)
  blocking collectives  34.7 us (13%)
  matrix products  32.3 us (12%)
  between operations  16.4 us (6%)
  local copies, waits for them, and re-layouts  13.6 us (5%)
  other arithmetic  5.5 us (2%)
    all_gather x2, waiting for transfers between devices, shards(): piece = lax.all_gather(loc, 'vpair', axis=1, tiled=True)  133 us
    all_to_all x1, blocking collectives, shards(): lax.all_to_all(cycle, 'vpair', split_axis=1, concat_axis=2, tiled=True)  34.7 us
    reduce_scatter x2, waiting for transfers between devices, shards(): lax.psum_scatter(part, 'opair', scatter_dimension=0, tiled=True)  28.7 us
    dot_general x2, matrix products, shards(): lax.dot_general(piece, v_slab, (((0, 2), (0, 1)), ((), ())), preferred_el...  26.7 us
    dot_general x1, matrix products, shards(): lax.dot_general(cycle_amps, cycle_ints, (((0, 1), (0, 1)), ((), ())), pre...  5.67 us
  transfers between devices with their start and end apart: 5, of which 3 were waited for; matrix products, arithmetic and copies ran while one was open for 14% of the time, Pallas kernels for 0%

commit v1 on v0

--- a/solution.py
+++ b/solution.py
@@ -50,7 +50,15 @@
             loc, _, cycle = lax.optimization_barrier((loc, prev, cycle))
         else:
             loc, _ = lax.optimization_barrier((loc, prev))
-        piece = lax.all_gather(loc, "vpair", axis=1, tiled=True)
+        piece = jnp.concatenate(
+            lax.all_to_all(
+                jnp.stack([loc] * lax.axis_size("vpair"), axis=0),
+                concat_axis=0,
+                split_axis=0,
+                axis_name="vpair",
+            ),
+            axis=1,
+        )
         prev = piece
         part = lax.dot_general(
             piece, v_slab, (((0, 2), (0, 1)), ((), ())), preferred_element_type=jnp.float32

time: 266 us -> 437 us (1.64)
  blocking collectives: 34.7 us -> 179 us
  local copies, waits for them, and re-layouts: 13.6 us -> 56.6 us
  waiting for transfers between devices: 162 us -> 146 us
  starting transfers between devices: 0.17 us -> 5.88 us
    all_to_all x0 -> x1, blocking collectives: none -> 152 us  [shards(): lax.all_to_all(jnp.stack([loc] * lax.axis_size('vpair'), axis=0), concat_...]
    all_gather x2 -> x0, waiting for transfers between devices: 133 us -> none  [shards(): piece = lax.all_gather(loc, 'vpair', axis=1, tiled=True)]
    all_to_all x0 -> x1, waiting for transfers between devices: none -> 118 us  [shards(): lax.all_to_all(jnp.stack([loc] * lax.axis_size('vpair'), axis=0), concat_...]
    reshape x0 -> x4, local copies, waits for them, and re-layouts: none -> 25 us  [shards(): jnp.concatenate(lax.all_to_all(jnp.stack([loc] * lax.axis_size('vpair'),...]
    dot_general x0 -> x2, local copies, waits for them, and re-layouts: none -> 13.5 us  [shards(): lax.dot_general(piece, v_slab, (((0, 2), (0, 1)), ((), ())), preferred_el...]
    all_to_all x1, blocking collectives: 34.7 us -> 27.5 us  [shards(): lax.all_to_all(cycle, 'vpair', split_axis=1, concat_axis=2, tiled=True)]
    all_to_all x0 -> x1, starting transfers between devices: none -> 5.61 us  [shards(): lax.all_to_all(jnp.stack([loc] * lax.axis_size('vpair'), axis=0), concat_...]
  transfers between devices with their start and end apart: 5 -> 4, of which waited for: 3 -> 2; matrix products, arithmetic and copies ran while one was open for 14% -> 16% of each run, Pallas kernels for 0% -> 0%
where the time goes in v1:
time: 437 us; the launch traced here: 436 us
  blocking collectives  179 us (41%)
  waiting for transfers between devices  146 us (33%)
  local copies, waits for them, and re-layouts  56.6 us (13%)
  matrix products  28 us (6%)
  between operations  14.5 us (3%)
  starting transfers between devices  5.88 us (1%)
  other arithmetic  5.5 us (1%)
    all_to_all x1, blocking collectives, shards(): lax.all_to_all(jnp.stack([loc] * lax.axis_size('vpair'), axis=0), concat_...  152 us
    all_to_all x1, waiting for transfers between devices, shards(): lax.all_to_all(jnp.stack([loc] * lax.axis_size('vpair'), axis=0), concat_...  118 us
    reduce_scatter x2, waiting for transfers between devices, shards(): lax.psum_scatter(part, 'opair', scatter_dimension=0, tiled=True)  28.8 us
    all_to_all x1, blocking collectives, shards(): lax.all_to_all(cycle, 'vpair', split_axis=1, concat_axis=2, tiled=True)  27.5 us
    reshape x4, local copies, waits for them, and re-layouts, shards(): jnp.concatenate(lax.all_to_all(jnp.stack([loc] * lax.axis_size('vpair'),...  25 us
    dot_general x2, matrix products, shards(): lax.dot_general(piece, v_slab, (((0, 2), (0, 1)), ((), ())), preferred_el...  22.3 us
    dot_general x2, local copies, waits for them, and re-layouts, shards(): lax.dot_general(piece, v_slab, (((0, 2), (0, 1)), ((), ())), preferred_el...  13.5 us
  transfers between devices with their start and end apart: 4, of which 2 were waited for; matrix products, arithmetic and copies ran while one was open for 16% of the time, Pallas kernels for 0%

profile of v1, /device:TPU:2, one launch (start us, length us, event | category | flops | bytes accessed | tf_op | source)
XLA Modules:
  0.0 436.2 jit_solution(7753704221787630505)
XLA Ops:
  6.5 1.2 slice_bitcast_fusion
  8.3 5.7 %fusion.13 = f32[512,3125,1]{1,0,2:T(8,128)} fusion(bf16[3,100,512]{2,1,0:T(8,128)(2,1)} %param.12, bf16[3,100,3125]{2,1,0:T(8,128)(2,1)S(1)} %copy-done), kind=kOutput, calls=%fused_computation.27 | convolution fusion | flops 960000000 | bytes 8582200 | tf_op jit(solution)/shard_map/dot_general | solution.py:34
  14.8 151.8 %all_to_all.22 = bf16[32,3,25,1000]{3,2,1,0:T(8,128)(2,1)S(1)} all-to-all(bf16[32,3,25,1000]{3,2,1,0:T(8,128)(2,1)S(1)} %stack.6), channel_id=1, replica_groups=mesh['opair'=8,'vpair'=32] {'vpair'}, dimensions={0} | all-to-all | bytes 9600000 | tf_op jit(solution)/shard_map/all_to_all | solution.py:54
  166.6 3.4 copy.37
  170.0 7.5 %reshape.201 = bf16[3,800,1000]{2,1,0:T(8,128)(2,1)} reshape(bf16[3,32,25,1000]{3,2,1,0:T(8,128)(2,1)} %copy.37) | data formatting | bytes 9600000 | tf_op jit(solution)/shard_map/reshape | solution.py:53
  177.4 1.8 copy.39
  179.2 27.5 %all_to_all.23 = f32[2,32,3125]{2,0,1:T(2,128)S(1)} all-to-all(f32[2,32,3125]{2,0,1:T(2,128)S(1)} %copy.39), channel_id=1, replica_groups=mesh['opair'=8,'vpair'=32] {'vpair'}, dimensions={1} | all-to-all | bytes 1600000 | tf_op jit(solution)/shard_map/all_to_all | solution.py:68
  206.7 3.5 stack.7
  210.1 5.6 %all-to-all-start.1 = ((bf16[32,3,25,1000]{3,2,1,0:T(8,128)(2,1)}), bf16[32,3,25,1000]{3,2,1,0:T(8,128)(2,1)}, u32[]{:S(2)}, u32[]{:S(2)}) async-start(bf16[32,3,25,1000]{3,2,1,0:T(8,128)(2,1)} %stack.7), calls=%async_computation.2 | async-start | bytes 12582912 | tf_op jit(solution)/shard_map/all_to_all | solution.py:54
  215.8 6.8 %dot_general.22 = bf16[16,50,3,1000]{3,1,0,2:T(8,128)(2,1)} reshape(bf16[800,3,1000]{2,0,1:T(8,128)(2,1)} %bitcast.53) | data formatting | bytes 9600000 | tf_op jit(solution)/shard_map/dot_general | solution.py:63
  222.6 11.1 %fusion.7 = f32[16,50,1000]{2,1,0:T(8,128)} fusion(bf16[16,50,3,1000]{3,1,0,2:T(8,128)(2,1)} %dot_general.22, bf16[3,1000,1,1000]{3,1,2,0:T(8,128)(2,1)} %param.11), kind=kOutput, calls=%fused_computation.5 | convolution fusion | flops 4800000000 | bytes 14000000 | tf_op jit(solution)/shard_map/dot_general | solution.py:63
  234.0 2.0 all_to_all.18
  236.0 117.6 %all-to-all-done.1 = bf16[32,3,25,1000]{3,2,1,0:T(8,128)(2,1)} async-done(((bf16[32,3,25,1000]{3,2,1,0:T(8,128)(2,1)}), bf16[32,3,25,1000]{3,2,1,0:T(8,128)(2,1)}, u32[]{:S(2)}, u32[]{:S(2)}) %all-to-all-start.1) | async-done | bytes 4800032 | tf_op jit(solution)/shard_map/all_to_all | solution.py:54
  353.5 6.8 %copy.38 = bf16[3,32,25,1000]{3,2,1,0:T(8,128)(2,1)} copy(bf16[3,32,25,1000]{3,2,0,1:T(8,128)(2,1)} %bitcast.11) | data formatting | bytes 9600000 | tf_op jit(solution)/shard_map/reshape | solution.py:53
  360.3 7.4 %reshape.203 = bf16[3,800,1000]{2,1,0:T(8,128)(2,1)} reshape(bf16[3,32,25,1000]{3,2,1,0:T(8,128)(2,1)} %copy.38) | data formatting | bytes 9600000 | tf_op jit(solution)/shard_map/reshape | solution.py:53
  367.7 6.7 %dot_general.19 = bf16[16,50,3,1000]{3,1,0,2:T(8,128)(2,1)} reshape(bf16[800,3,1000]{2,0,1:T(8,128)(2,1)} %bitcast.54) | data formatting | bytes 9600000 | tf_op jit(solution)/shard_map/dot_general | solution.py:63
  374.5 11.2 %fusion.4 = f32[16,50,1000]{2,1,0:T(8,128)} fusion(bf16[16,50,3,1000]{3,1,0,2:T(8,128)(2,1)} %dot_general.19, bf16[3,1000,1,1000]{3,1,2,0:T(8,128)(2,1)} %param.11), kind=kOutput, calls=%fused_computation.4 | convolution fusion | flops 4800000000 | bytes 14000000 | tf_op jit(solution)/shard_map/dot_general | solution.py:63
  390.8 2.2 copy.41
  393.0 2.2 reshape.205
  395.2 28.8 %reduce-scatter.8.cloned.1.call-done = f32[2,50,1000]{2,1,0:T(8,128)} async-done(((f32[16,50,1000]{2,1,0:T(8,128)}), f32[2,50,1000]{2,1,0:T(8,128)}) %reduce-scatter.8.cloned.1.call-update) | async-done | bytes 400016 | tf_op jit(solution)/shard_map/reduce_scatter | solution.py:72
  424.0 1.3 copy.42
  425.3 1.4 pad_maximum_fusion
  426.8 1.1 compare_select_fusion
  427.9 1.7 copy.45
  (36 shorter events, 5.4 us)
Async XLA Ops:
  6.5 1.7 copy-start
  6.5 170.9 %reduce-scatter.4.cloned.1.call-start = ((), (), s32[]{:S(2)}) async-start(), calls=%async_computation.6 | async-start | bytes 7372800 | tf_op jit(solution)/shard_map/reduce_scatter | solution.py:48
  210.1 143.4 %all-to-all-start.1 = ((bf16[32,3,25,1000]{3,2,1,0:T(8,128)(2,1)}), bf16[32,3,25,1000]{3,2,1,0:T(8,128)(2,1)}, u32[]{:S(2)}, u32[]{:S(2)}) async-start(bf16[32,3,25,1000]{3,2,1,0:T(8,128)(2,1)} %stack.7), calls=%async_computation.2 | async-start | bytes 12582912 | tf_op jit(solution)/shard_map/all_to_all | solution.py:54
  215.8 169.9 %reduce-scatter.6.cloned.1.call-start = ((), (), s32[]{:S(2)}) async-start(), calls=%async_computation.7 | async-start | bytes 4128768 | tf_op jit(solution)/shard_map/reduce_scatter | solution.py:72
  233.7 190.3 %reduce-scatter.8.cloned.1.call-start = ((), (), s32[]{:S(2)}) async-start(), calls=%async_computation.8 | async-start | bytes 4128768 | tf_op jit(solution)/shard_map/reduce_scatter | solution.py:72
  374.5 12.6 %copy-start.4 = (s32[8]{0:T(128)S(1)}, s32[8]{0:T(128)}, u32[]{:S(2)}) copy-start(s32[8]{0:T(128)} %param.14) | copy-start | bytes 100
  374.5 12.8 %copy-start.5 = (s32[8]{0:T(128)S(1)}, s32[8]{0:T(128)}, u32[]{:S(2)}) copy-start(s32[8]{0:T(128)} %param.15) | copy-start | bytes 100
  374.5 12.9 %copy-start.2 = (f32[1000]{0:T(1024)S(1)}, f32[1000]{0:T(1024)}, u32[]{:S(2)}) copy-start(f32[1000]{0:T(1024)} %param.19) | copy-start | bytes 12004
  374.5 13.6 %copy-start.3 = (f32[100]{0:T(128)S(1)}, f32[100]{0:T(128)}, u32[]{:S(2)}) copy-start(f32[100]{0:T(128)} %param.18) | copy-start | bytes 1204
  390.6 39.0 %copy-start.1 = (bf16[3,100,3125]{2,1,0:T(8,128)(2,1)S(1)}, bf16[3,100,3125]{2,1,0:T(8,128)(2,1)}, u32[]{:S(2)}) copy-start(bf16[3,100,3125]{2,1,0:T(8,128)(2,1)} %param.13) | copy-start | bytes 5625004
Sparse Core Ops, SparseCore 0:
  14.1 49.2 reduce-scatter.3
  233.8 41.5 reduce-scatter.5
  385.8 38.0 reduce-scatter.7
